TPU v7x, 32 devices: a whole 2x2x4 slice. The times are simulated.
32 devices in a mesh: dp: 8 (over z, y), seq: 4 (over x, core).
Axes of the slice: x: 2, y: 2, z: 4, core: 2. Of those that a mesh axis runs over, the one named last changes fastest.
Arguments:
- frames: bfloat16 [8, 512, 1536], P('dp', 'seq'), may hold values from -6 to 6
- lengths: int32 [8, 4], P('dp'), may hold values from 1 to 256, 512 in all within a row
- ln1_gain: float32 [1536], replicated, may hold values from 0.5 to 12
- ln2_gain: float32 [1536], replicated, may hold values from 0.5 to 1.5
- w_qkv: bfloat16 [1536, 3, 1536], P('dp', None, 'seq'), may hold values from -0.15625 to 0.15625
- w_out: bfloat16 [1536, 1536], P('seq', 'dp'), may hold values from -0.15625 to 0.15625
- w_glu: bfloat16 [1536, 2, 1536], P('dp', None, 'seq'), may hold values from -0.15625 to 0.15625
- dw_kernel: bfloat16 [31, 1536], P(None, 'seq'), may hold values from -1 to 1
- w_proj: bfloat16 [1536, 1536], P('seq', 'dp'), may hold values from -0.15625 to 0.15625
Outputs:
- block_out: bfloat16 [8, 512, 1536], P('dp', 'seq')
Inputs may be any that keep to these rules, and one draw needn't show every extreme that they name: `lengths`: each row sums to 512, and its largest entry is 256.
All inputs are finite; a program needn't handle non-finite values.
Results may differ from a plain program's by a relative error of at most 0.013.
The roundings to bfloat16 on the way count: a program that leaves them out, or rounds other values in their place, can miss the bound.
Values may be sent and summed in bfloat16 or wider, within the bound.
No kernel may reach another device: no remote copies, remote signals or barrier semaphores. Data moves between devices by JAX's collectives and lax.ppermute only.
A program may use at most 64 MiB of HBM per device.

v0:
```python
import jax
import jax.numpy as jnp
from jax import lax
from jax.sharding import PartitionSpec as P

HD = 96


def layer_norm(values, gain_vec):
    mean_value = jnp.mean(values, axis=-1, keepdims=True)
    centered = values - mean_value
    variance = jnp.mean(centered * centered, axis=-1, keepdims=True)
    return (centered * lax.rsqrt(variance + 1e-05) * gain_vec).astype(jnp.bfloat16)


def segment_of(record_ends, positions):
    return jnp.sum((positions[:, None] >= record_ends[None, :]).astype(jnp.int32), axis=1)


def attend(projected, seg_all, head_size):
    group_rows = projected.shape[0]
    block_rows = 512
    heads_here = projected.shape[2] // head_size
    split = projected.reshape(group_rows, 3, heads_here, head_size)
    queries = split[:, 0]
    keys = split[:, 1]
    values = split[:, 2]
    blocks = group_rows // block_rows
    scale = 1.0 / head_size**0.5

    def one_block(block_data):
        query_block, seg_block = block_data
        scores = (
            jnp.einsum("qhe,khe->hqk", query_block, keys, preferred_element_type=jnp.float32)
            * scale
        )
        allowed = seg_block[:, None] == seg_all[None, :]
        scores = jnp.where(allowed[None], scores, -1e30)
        top_score = jnp.max(scores, axis=-1, keepdims=True)
        weights = jnp.exp(scores - top_score)
        probs = (weights / jnp.sum(weights, axis=-1, keepdims=True)).astype(jnp.bfloat16)
        mixed = jnp.einsum("hqk,khe->qhe", probs, values, preferred_element_type=jnp.float32)
        return mixed.astype(jnp.bfloat16).reshape(block_rows, heads_here * head_size)

    result = lax.map(
        one_block,
        (
            queries.reshape(blocks, block_rows, heads_here, head_size),
            seg_all.reshape(blocks, block_rows),
        ),
    )
    return result.reshape(group_rows, heads_here * head_size)


def depthwise(padded, kernel, seg_here, seg_near, count):
    total_acc = jnp.zeros((count, padded.shape[1]), jnp.float32)
    for tap_index in range(kernel.shape[0]):
        window = padded[tap_index : tap_index + count].astype(jnp.float32)
        same = (seg_near[tap_index : tap_index + count] == seg_here)[:, None]
        total_acc = total_acc + jnp.where(same, window * kernel[tap_index].astype(jnp.float32), 0.0)
    return jax.nn.silu(total_acc).astype(jnp.bfloat16)


def on_device(frames, lengths, ln1_gain, ln2_gain, w_qkv, w_out, w_glu, dw_kernel, w_proj):
    frame_rows = frames.shape[1]
    model_width = frames.shape[2]
    seq_count = lax.axis_size("seq")
    group_rows = frame_rows * seq_count
    group_width = model_width // seq_count
    kernel_reach = dw_kernel.shape[0] // 2
    qkv_local = lax.all_gather(w_qkv, "dp", axis=0, tiled=True)
    out_local = lax.all_gather(w_out, "dp", axis=1, tiled=True)
    glu_local = lax.all_gather(w_glu, "dp", axis=0, tiled=True)
    proj_local = lax.all_gather(w_proj, "dp", axis=1, tiled=True)
    qkv_matrix = qkv_local.reshape(model_width, 3 * group_width)
    glu_matrix = glu_local.reshape(model_width, 2 * group_width)
    inputs = frames[0].astype(jnp.float32)
    record_ends = jnp.cumsum(lengths[0])
    seg_all = segment_of(record_ends, jnp.arange(group_rows, dtype=jnp.int32))
    normed1 = layer_norm(inputs, ln1_gain)
    projected = (
        jnp.dot(
            lax.all_gather(normed1, "seq", axis=0, tiled=True),
            qkv_matrix,
            preferred_element_type=jnp.float32,
        )
        .astype(jnp.bfloat16)
        .reshape(group_rows, 3, group_width)
    )
    attended = attend(projected, seg_all, HD)
    rows_here = attended
    attn_sum = lax.psum_scatter(
        jnp.dot(rows_here, out_local, preferred_element_type=jnp.float32)
        .astype(jnp.bfloat16)
        .astype(jnp.float32)
        .astype(jnp.bfloat16),
        "seq",
        scatter_dimension=0,
        tiled=True,
    ).astype(jnp.float32)
    middle = (inputs + attn_sum).astype(jnp.bfloat16)
    normed2 = layer_norm(middle.astype(jnp.float32), ln2_gain)
    shard_piece = lax.all_gather(normed2, "seq", axis=0, tiled=True)
    paired = jnp.dot(shard_piece, glu_matrix, preferred_element_type=jnp.float32).reshape(
        shard_piece.shape[0], 2, group_width
    )
    gated = (paired[:, 0] * jax.nn.sigmoid(paired[:, 1])).astype(jnp.bfloat16)
    padded = jnp.pad(gated, ((kernel_reach, kernel_reach), (0, 0)))
    near_positions = jnp.arange(-kernel_reach, group_rows + kernel_reach, dtype=jnp.int32)
    activated = depthwise(
        padded, dw_kernel, seg_all, segment_of(record_ends, near_positions), group_rows
    )
    rows_here = activated
    conv_out = lax.psum_scatter(
        jnp.dot(rows_here, proj_local, preferred_element_type=jnp.float32)
        .astype(jnp.bfloat16)
        .astype(jnp.float32)
        .astype(jnp.bfloat16),
        "seq",
        scatter_dimension=0,
        tiled=True,
    ).astype(jnp.float32)
    results = [(middle.astype(jnp.float32) + conv_out).astype(jnp.bfloat16)]
    return jnp.stack(results, axis=0)


def solution(mesh):
    in_specs = (
        P("dp", "seq", None),
        P("dp", None),
        P(),
        P(),
        P("dp", None, "seq"),
        P("seq", "dp"),
        P("dp", None, "seq"),
        P(None, "seq"),
        P("seq", "dp"),
    )
    out_specs = P("dp", "seq", None)
    return jax.shard_map(
        on_device, mesh=mesh, in_specs=in_specs, out_specs=out_specs, check_vma=False
    )
```

profile of v0, /device:TPU:0, one launch (start us, length us, event | category | flops | bytes accessed | tf_op | source)
XLA Modules:
  0.0 334.3 jit_solution(194160202395441783)
XLA Ops:
  6.5 0.0 copy-start.3
  6.5 0.0 all-gather.9.cloned.1.call-start
  6.5 0.7 all-gather.9.cloned.1.call-update
  7.3 0.0 all-gather.7.cloned.1.call-start
  7.3 1.1 convert_reduce_fusion.1
  8.4 1.2 fusion.19
  9.7 2.0 fusion.21
  11.7 0.0 all-gather.7.cloned.1.call-update
  11.8 0.0 all-gather.11.cloned.1.call-start
  11.8 0.7 all-gather.11.cloned.1.call-update
  12.5 0.0 reduce-scatter.3.cloned.1.call-start
  12.5 0.0 copy-done.3
  12.6 0.2 reduce-window.8
  12.7 0.1 convert_reduce_fusion.3
  12.8 0.2 broadcast_compare_fusion
  13.0 64.4 %all-gather.9.cloned.1.call-done = bf16[1536,3,384]{2,0,1:T(8,128)(2,1)} async-done(((bf16[192,3,384]{2,0,1:T(8,128)(2,1)}), bf16[1536,3,384]{2,0,1:T(8,128)(2,1)}) %all-gather.9.cloned.1.call-update) | async-done | bytes 3538960 | tf_op jit(solution)/shard_map/all_gather | solution.py:71
  77.5 6.1 %copy.23 = bf16[1536,3,384]{0,2,1:T(8,128)(2,1)} copy(bf16[1536,3,384]{2,0,1:T(8,128)(2,1)} %all-gather.9.cloned.1.call-done) | data formatting | bytes 7077888 | tf_op jit(solution)/shard_map/all_gather | solution.py:71
  83.6 13.6 %all-gather.7.cloned.1.call-done = bf16[512,1536]{1,0:T(8,128)(2,1)} async-done(((bf16[128,1536]{1,0:T(8,128)(2,1)}), bf16[512,1536]{1,0:T(8,128)(2,1)}) %all-gather.7.cloned.1.call-update) | async-done | bytes 1572880 | tf_op jit(solution)/shard_map/all_gather | solution.py:83
  97.2 4.7 %convolution_convert_fusion = bf16[512,1152]{1,0:T(8,128)(2,1)S(1)} fusion(bf16[512,1536]{1,0:T(8,128)(2,1)} %all-gather.7.cloned.1.call-done, bf16[1536,1152]{0,1:T(8,128)(2,1)} %bitcast.70), kind=kOutput, calls=%fused_computation.5 | convolution fusion | flops 1812529152 | bytes 6291456 | tf_op jit(solution)/shard_map/dot_general | solution.py:82
  101.9 0.6 copy.24
  102.5 3.6 %fusion.40 = (f32[4,512]{1,0:T(4,128)S(1)}, f32[4,512,512]{1,2,0:T(8,128)}) fusion(pred[512,512]{0,1:T(8,128)(4,1)S(1)} %broadcast_compare_fusion, bf16[512,3,4,96]{0,3,2,1:T(8,128)(2,1)S(1)} %bitcast.71), kind=kOutput, calls=%fused_computation.130 | convolution fusion | flops 205521408 | bytes 5251072 | tf_op jit(solution)/shard_map/while/body/eval_jaxpr/sub | solution.py:40
  106.2 2.8 fusion.9
  108.9 31.5 %all-gather.11.cloned.1.call-done = bf16[384,1536]{0,1:T(8,128)(2,1)} async-done(((bf16[384,192]{0,1:T(8,128)(2,1)}), bf16[384,1536]{0,1:T(8,128)(2,1)}) %all-gather.11.cloned.1.call-update) | async-done | bytes 1179664 | tf_op jit(solution)/shard_map/all_gather | solution.py:72
  140.5 3.5 %convolution_convert_fusion.2 = bf16[512,1536]{1,0:T(8,128)(2,1)} fusion(bf16[512,384]{0,1:T(8,128)(2,1)S(1)} %bitcast.73, bf16[384,1536]{0,1:T(8,128)(2,1)} %all-gather.11.cloned.1.call-done), kind=kOutput, calls=%fused_computation.7 | convolution fusion | flops 604766208 | bytes 3145728 | tf_op jit(solution)/shard_map/dot_general | solution.py:93
  144.0 0.0 copy-start
  144.0 0.0 copy-start.2
  144.0 0.0 reduce-scatter.3.cloned.1.call-update
  144.0 0.0 copy-start.1
  144.0 0.0 all-gather.15.cloned.1.call-start
  144.0 0.5 all-gather.15.cloned.1.call-update
  144.6 0.0 all-gather.13.cloned.1.call-start
  144.6 26.5 %reduce-scatter.3.cloned.1.call-done = bf16[128,1536]{1,0:T(8,128)(2,1)} async-done(((bf16[512,1536]{1,0:T(8,128)(2,1)}), bf16[128,1536]{1,0:T(8,128)(2,1)}) %reduce-scatter.3.cloned.1.call-update) | async-done | bytes 393232 | tf_op jit(solution)/shard_map/reduce_scatter | solution.py:92
  171.1 0.0 copy-done
  171.1 1.2 convert_reduce_fusion
  172.3 0.3 fusion.16
  172.6 0.0 copy-done.2
  172.6 1.0 fusion.18
  173.6 0.0 all-gather.13.cloned.1.call-update
  173.6 0.0 all-gather.17.cloned.1.call-start
  173.7 0.7 all-gather.17.cloned.1.call-update
  174.4 0.0 reduce-scatter.5.cloned.1.call-start
  174.4 0.1 convert_reduce_fusion.2
  174.5 0.0 copy-done.1
  174.5 0.1 convert_reduce_fusion.33
  174.6 0.1 convert_reduce_fusion.34
  174.7 0.1 slice_compare_fusion.29
  174.8 0.1 slice_compare_fusion.30
  174.9 50.6 %all-gather.15.cloned.1.call-done = bf16[1536,2,384]{2,1,0:T(2,128)(2,1)} async-done(((bf16[192,2,384]{2,1,0:T(2,128)(2,1)}), bf16[1536,2,384]{2,1,0:T(2,128)(2,1)}) %all-gather.15.cloned.1.call-update) | async-done | bytes 2359312 | tf_op jit(solution)/shard_map/all_gather | solution.py:73
  225.5 5.6 %copy.28 = bf16[1536,2,384]{0,2,1:T(8,128)(2,1)S(1)} copy(bf16[1536,2,384]{2,1,0:T(2,128)(2,1)} %all-gather.15.cloned.1.call-done) | data formatting | bytes 4718592 | tf_op jit(solution)/shard_map/reshape | solution.py:76
  231.1 14.1 %all-gather.13.cloned.1.call-done = bf16[512,1536]{1,0:T(8,128)(2,1)} async-done(((bf16[128,1536]{1,0:T(8,128)(2,1)}), bf16[512,1536]{1,0:T(8,128)(2,1)}) %all-gather.13.cloned.1.call-update) | async-done | bytes 1572880 | tf_op jit(solution)/shard_map/all_gather | solution.py:103
  245.2 2.8 fusion.2
  248.0 0.2 fusion.32
  248.2 40.5 %all-gather.17.cloned.1.call-done = bf16[384,1536]{0,1:T(8,128)(2,1)} async-done(((bf16[384,192]{0,1:T(8,128)(2,1)}), bf16[384,1536]{0,1:T(8,128)(2,1)}) %all-gather.17.cloned.1.call-update) | async-done | bytes 1179664 | tf_op jit(solution)/shard_map/all_gather | solution.py:74
  288.7 9.8 %convolution_convert_fusion.1 = bf16[512,1536]{1,0:T(8,128)(2,1)} fusion(bf16[384,1536]{0,1:T(8,128)(2,1)} %all-gather.17.cloned.1.call-done, bf16[512,384]{1,0:T(8,128)(2,1)S(1)} %fusion.32, f32[384]{0:T(512)S(1)} %get-tuple-element.55, f32[384]{0:T(512)S(1)} %get-tuple-element.56, f32[384]{0:T(512)S(1)} %get-tuple-element.18, ...), kind=kOutput, calls=%fused_computation.6 | convolution fusion | flops 629932032 | bytes 3209216 | tf_op jit(solution)/shard_map/dot_general | solution.py:115
  298.5 0.0 reduce-scatter.5.cloned.1.call-update
  298.5 27.1 %reduce-scatter.5.cloned.1.call-done = bf16[128,1536]{1,0:T(8,128)(2,1)} async-done(((bf16[512,1536]{1,0:T(8,128)(2,1)}), bf16[128,1536]{1,0:T(8,128)(2,1)}) %reduce-scatter.5.cloned.1.call-update) | async-done | bytes 393232 | tf_op jit(solution)/shard_map/reduce_scatter | solution.py:114
  325.6 1.8 fusion.31
  (5 shorter events, 0.0 us)
Async XLA Ops:
  6.5 6.0 %copy-start.3 = (s32[1,4]{1,0:T(1,128)S(1)}, s32[1,4]{1,0:T(1,128)}, u32[]{:S(2)}) copy-start(s32[1,4]{1,0:T(1,128)} %param.10) | copy-start | bytes 52
  6.5 70.9 %all-gather.9.cloned.1.call-start = ((), (), s32[]{:S(2)}) async-start(), calls=%async_computation.3 | async-start | bytes 3981312 | tf_op jit(solution)/shard_map/all_gather | solution.py:71
  7.3 89.9 %all-gather.7.cloned.1.call-start = ((), (), s32[]{:S(2)}) async-start(), calls=%async_computation.2 | async-start | bytes 1966080 | tf_op jit(solution)/shard_map/all_gather | solution.py:83
  11.8 128.7 %all-gather.11.cloned.1.call-start = ((), (), s32[]{:S(2)}) async-start(), calls=%async_computation.4 | async-start | bytes 1327104 | tf_op jit(solution)/shard_map/all_gather | solution.py:72
  12.5 158.6 %reduce-scatter.3.cloned.1.call-start = ((), (), s32[]{:S(2)}) async-start(), calls=%async_computation.5 | async-start | bytes 1966080 | tf_op jit(solution)/shard_map/reduce_scatter | solution.py:92
  144.0 27.1 %copy-start = (bf16[1,128,1536]{2,1,0:T(8,128)(2,1)S(1)}, bf16[1,128,1536]{2,1,0:T(8,128)(2,1)}, u32[]{:S(2)}) copy-start(bf16[1,128,1536]{2,1,0:T(8,128)(2,1)} %param.9) | copy-start | bytes 1179652
  144.0 28.6 %copy-start.2 = (f32[1536]{0:T(1024)S(1)}, f32[1536]{0:T(1024)}, u32[]{:S(2)}) copy-start(f32[1536]{0:T(1024)} %param.12) | copy-start | bytes 18436
  144.0 30.5 %copy-start.1 = (bf16[31,384]{1,0:T(8,128)(2,1)S(1)}, bf16[31,384]{1,0:T(8,128)(2,1)}, u32[]{:S(2)}) copy-start(bf16[31,384]{1,0:T(8,128)(2,1)} %param.16) | copy-start | bytes 71428
  144.0 81.5 %all-gather.15.cloned.1.call-start = ((), (), s32[]{:S(2)}) async-start(), calls=%async_computation.7 | async-start | bytes 2654208 | tf_op jit(solution)/shard_map/all_gather | solution.py:73
  144.6 100.6 %all-gather.13.cloned.1.call-start = ((), (), s32[]{:S(2)}) async-start(), calls=%async_computation.6 | async-start | bytes 1966080 | tf_op jit(solution)/shard_map/all_gather | solution.py:103
  173.6 115.1 %all-gather.17.cloned.1.call-start = ((), (), s32[]{:S(2)}) async-start(), calls=%async_computation.8 | async-start | bytes 1327104 | tf_op jit(solution)/shard_map/all_gather | solution.py:74
  174.4 151.3 %reduce-scatter.5.cloned.1.call-start = ((), (), s32[]{:S(2)}) async-start(), calls=%async_computation.9 | async-start | bytes 1966080 | tf_op jit(solution)/shard_map/reduce_scatter | solution.py:114
Sparse Core Ops, SparseCore 0:
  9.5 67.8 all-gather.8
  79.0 18.1 all-gather.6
  99.4 41.0 all-gather.10
  144.1 26.9 reduce-scatter.2
  173.3 52.0 all-gather.14
  227.0 18.1 all-gather.12
  247.6 41.0 all-gather.16
  298.7 26.9 reduce-scatter.4
where the time goes:
time: 335 us; the launch traced here: 334 us
  waiting for transfers between devices  271 us (81%)
  matrix products  27.2 us (8%)
  between operations  13.6 us (4%)
  local copies, waits for them, and re-layouts  12.4 us (4%)
  other arithmetic  9.88 us (3%)
    all_gather x1, waiting for transfers between devices, on_device(): qkv_local = lax.all_gather(w_qkv, 'dp', axis=0, tiled=True)  64.4 us
    all_gather x1, waiting for transfers between devices, on_device(): glu_local = lax.all_gather(w_glu, 'dp', axis=0, tiled=True)  50.6 us
    all_gather x1, waiting for transfers between devices, on_device(): proj_local = lax.all_gather(w_proj, 'dp', axis=1, tiled=True)  40.5 us
    all_gather x1, waiting for transfers between devices, on_device(): out_local = lax.all_gather(w_out, 'dp', axis=1, tiled=True)  31.5 us
    reduce_scatter x1, waiting for transfers between devices, on_device(): lax.psum_scatter(jnp.dot(rows_here, proj_local, preferred_element_type=jn...  27.1 us
    reduce_scatter x1, waiting for transfers between devices, on_device(): lax.psum_scatter(jnp.dot(rows_here, out_local, preferred_element_type=jnp...  26.5 us
    all_gather x1, waiting for transfers between devices, on_device(): shard_piece = lax.all_gather(normed2, 'seq', axis=0, tiled=True)  14.1 us
    all_gather x1, waiting for transfers between devices, on_device(): lax.all_gather(normed1, 'seq', axis=0, tiled=True)  13.6 us
  transfers between devices with their start and end apart: 8, of which 8 were waited for; matrix products, arithmetic and copies ran while one was open for 10% of the time, Pallas kernels for 0%

commit v1 on v0

--- a/solution.py
+++ b/solution.py
@@ -4,6 +4,16 @@
 from jax.sharding import PartitionSpec as P
 
 HD = 96
+
+
+def gather_by_hops(x, axis, dim):
+    size = lax.axis_size(axis)
+    held, pieces = (x, [x])
+    for _ in range(size - 1):
+        held = lax.ppermute(held, axis, [(i, (i + 1) % size) for i in range(size)])
+        pieces.insert(0, held)
+    merged = jnp.concatenate(pieces, axis=dim)
+    return jnp.roll(merged, (lax.axis_index(axis) + 1) * x.shape[dim], axis=dim)
 
 
 def layer_norm(values, gain_vec):
@@ -70,7 +80,7 @@
     kernel_reach = dw_kernel.shape[0] // 2
     qkv_local = lax.all_gather(w_qkv, "dp", axis=0, tiled=True)
     out_local = lax.all_gather(w_out, "dp", axis=1, tiled=True)
-    glu_local = lax.all_gather(w_glu, "dp", axis=0, tiled=True)
+    glu_local = gather_by_hops(w_glu, "dp", 0)
     proj_local = lax.all_gather(w_proj, "dp", axis=1, tiled=True)
     qkv_matrix = qkv_local.reshape(model_width, 3 * group_width)
     glu_matrix = glu_local.reshape(model_width, 2 * group_width)

time: 335 us -> 328 us (0.979)
  waiting for transfers between devices: 271 us -> 254 us
  other arithmetic: 9.88 us -> 13.3 us
    ppermute x0 -> x7, waiting for transfers between devices: none -> 90.3 us  [gather_by_hops(): held = lax.ppermute(held, axis, [(i, (i + 1) % size) for i in range(size)])]
    all_gather x1 -> x0, waiting for transfers between devices: 50.6 us -> none  [on_device(): glu_local = lax.all_gather(w_glu, 'dp', axis=0, tiled=True)]
    all_gather x1, waiting for transfers between devices: 40.5 us -> 0.02 us  [on_device(): proj_local = lax.all_gather(w_proj, 'dp', axis=1, tiled=True)]
    all_gather x1, waiting for transfers between devices: 14.1 us -> 0.01 us  [on_device(): shard_piece = lax.all_gather(normed2, 'seq', axis=0, tiled=True)]
    concatenate x0 -> x1, local copies, waits for them, and re-layouts: none -> 8.07 us  [gather_by_hops(): return jnp.roll(merged, (lax.axis_index(axis) + 1) * x.shape[dim], axis=dim)]
    reshape x1 -> x0, local copies, waits for them, and re-layouts: 5.64 us -> none  [on_device(): glu_matrix = glu_local.reshape(model_width, 2 * group_width)]
  transfers between devices with their start and end apart: 8 -> 14, of which waited for: 8 -> 12; matrix products, arithmetic and copies ran while one was open for 10% -> 12% of each run, Pallas kernels for 0% -> 0%
where the time goes in v1:
time: 328 us; the launch traced here: 327 us
  waiting for transfers between devices  254 us (77%)
  matrix products  28.8 us (9%)
  local copies, waits for them, and re-layouts  15.5 us (5%)
  between operations  14 us (4%)
  other arithmetic  13.3 us (4%)
    ppermute x7, waiting for transfers between devices, gather_by_hops(): held = lax.ppermute(held, axis, [(i, (i + 1) % size) for i in range(size)])  90.3 us
    all_gather x1, waiting for transfers between devices, on_device(): qkv_local = lax.all_gather(w_qkv, 'dp', axis=0, tiled=True)  64.4 us
    all_gather x1, waiting for transfers between devices, on_device(): out_local = lax.all_gather(w_out, 'dp', axis=1, tiled=True)  31.6 us
    reduce_scatter x1, waiting for transfers between devices, on_device(): lax.psum_scatter(jnp.dot(rows_here, out_local, preferred_element_type=jnp...  27 us
    reduce_scatter x1, waiting for transfers between devices, on_device(): lax.psum_scatter(jnp.dot(rows_here, proj_local, preferred_element_type=jn...  25.3 us
    all_gather x1, waiting for transfers between devices, on_device(): lax.all_gather(normed1, 'seq', axis=0, tiled=True)  13.6 us
    dot_general x1, matrix products, on_device(): jnp.dot(rows_here, proj_local, preferred_element_type=jnp.float32)  10.5 us
    concatenate x1, local copies, waits for them, and re-layouts, gather_by_hops(): return jnp.roll(merged, (lax.axis_index(axis) + 1) * x.shape[dim], axis=dim)  8.07 us
  transfers between devices with their start and end apart: 14, of which 12 were waited for; matrix products, arithmetic and copies ran while one was open for 12% of the time, Pallas kernels for 0%

profile of v1, /device:TPU:0, one launch (start us, length us, event | category | flops | bytes accessed | tf_op | source)
XLA Modules:
  0.0 327.1 jit_solution(2715544496995799083)
XLA Ops:
  6.5 0.7 all-gather.8.cloned.1.call-update
  7.3 0.0 all-gather.6.cloned.1.call-start
  7.3 1.1 convert_reduce_fusion.1
  8.4 1.2 fusion.20
  9.7 2.0 fusion.22
  11.7 0.0 all-gather.6.cloned.1.call-update
  11.8 0.0 all-gather.10.cloned.1.call-start
  11.8 0.7 all-gather.10.cloned.1.call-update
  12.5 0.0 reduce-scatter.3.cloned.1.call-start
  12.6 0.2 reduce-window.8
  12.7 0.1 convert_reduce_fusion.3
  12.8 0.2 broadcast_compare_fusion
  13.0 64.4 %all-gather.8.cloned.1.call-done = bf16[1536,3,384]{2,0,1:T(8,128)(2,1)} async-done(((bf16[192,3,384]{2,0,1:T(8,128)(2,1)}), bf16[1536,3,384]{2,0,1:T(8,128)(2,1)}) %all-gather.8.cloned.1.call-update) | async-done | bytes 3538960 | tf_op jit(solution)/shard_map/all_gather | solution.py:81
  77.5 6.1 %copy.26 = bf16[1536,3,384]{0,2,1:T(8,128)(2,1)} copy(bf16[1536,3,384]{2,0,1:T(8,128)(2,1)} %all-gather.8.cloned.1.call-done) | data formatting | bytes 7077888 | tf_op jit(solution)/shard_map/all_gather | solution.py:81
  83.6 13.6 %all-gather.6.cloned.1.call-done = bf16[512,1536]{1,0:T(8,128)(2,1)} async-done(((bf16[128,1536]{1,0:T(8,128)(2,1)}), bf16[512,1536]{1,0:T(8,128)(2,1)}) %all-gather.6.cloned.1.call-update) | async-done | bytes 1572880 | tf_op jit(solution)/shard_map/all_gather | solution.py:93
  97.2 4.7 %convolution_convert_fusion = bf16[512,1152]{1,0:T(8,128)(2,1)S(1)} fusion(bf16[512,1536]{1,0:T(8,128)(2,1)} %all-gather.6.cloned.1.call-done, bf16[1536,1152]{0,1:T(8,128)(2,1)} %bitcast.70), kind=kOutput, calls=%fused_computation.5 | convolution fusion | flops 1812529152 | bytes 6291456 | tf_op jit(solution)/shard_map/dot_general | solution.py:92
  101.9 0.6 copy.27
  102.5 3.6 %fusion.42 = (f32[4,512]{1,0:T(4,128)S(1)}, f32[4,512,512]{1,2,0:T(8,128)}) fusion(pred[512,512]{0,1:T(8,128)(4,1)S(1)} %broadcast_compare_fusion, bf16[512,3,4,96]{0,3,2,1:T(8,128)(2,1)S(1)} %bitcast.71), kind=kOutput, calls=%fused_computation.132 | convolution fusion | flops 205521408 | bytes 5251072 | tf_op jit(solution)/shard_map/while/body/eval_jaxpr/sub | solution.py:50
  106.2 2.8 fusion.10
  108.9 31.6 %all-gather.10.cloned.1.call-done = bf16[384,1536]{0,1:T(8,128)(2,1)} async-done(((bf16[384,192]{0,1:T(8,128)(2,1)}), bf16[384,1536]{0,1:T(8,128)(2,1)}) %all-gather.10.cloned.1.call-update) | async-done | bytes 1179664 | tf_op jit(solution)/shard_map/all_gather | solution.py:82
  140.5 3.5 %convolution_convert_fusion.2 = bf16[512,1536]{1,0:T(8,128)(2,1)} fusion(bf16[512,384]{0,1:T(8,128)(2,1)S(1)} %bitcast.73, bf16[384,1536]{0,1:T(8,128)(2,1)} %all-gather.10.cloned.1.call-done), kind=kOutput, calls=%fused_computation.7 | convolution fusion | flops 604766208 | bytes 3145728 | tf_op jit(solution)/shard_map/dot_general | solution.py:103
  144.0 0.0 reduce-scatter.3.cloned.1.call-update
  144.0 0.0 all-gather.12.cloned.1.call-start
  144.0 27.0 %reduce-scatter.3.cloned.1.call-done = bf16[128,1536]{1,0:T(8,128)(2,1)} async-done(((bf16[512,1536]{1,0:T(8,128)(2,1)}), bf16[128,1536]{1,0:T(8,128)(2,1)}) %reduce-scatter.3.cloned.1.call-update) | async-done | bytes 393232 | tf_op jit(solution)/shard_map/reduce_scatter | solution.py:102
  171.1 1.2 convert_reduce_fusion
  172.3 0.3 fusion.17
  172.6 1.0 fusion.19
  173.6 0.0 all-gather.12.cloned.1.call-update
  173.6 0.0 all-gather.14.cloned.1.call-start
  173.7 0.3 copy.29
  173.9 1.5 collective-permute-start
  175.5 12.1 %collective-permute-done = bf16[192,2,384]{0,2,1:T(8,128)(2,1)S(1)} collective-permute-done((bf16[192,2,384]{0,2,1:T(8,128)(2,1)S(1)}, bf16[192,2,384]{0,2,1:T(8,128)(2,1)S(1)}, u32[]{:S(2)}, u32[]{:S(2)}) %collective-permute-start) | collective-permute-done | bytes 294944 | tf_op jit(solution)/shard_map/ppermute | solution.py:13
  187.5 12.6 %collective-permute-done.1 = bf16[192,2,384]{0,2,1:T(8,128)(2,1)S(1)} collective-permute-done((bf16[192,2,384]{0,2,1:T(8,128)(2,1)S(1)}, bf16[192,2,384]{0,2,1:T(8,128)(2,1)S(1)}, u32[]{:S(2)}, u32[]{:S(2)}) %collective-permute-start.1) | collective-permute-done | bytes 294944 | tf_op jit(solution)/shard_map/ppermute | solution.py:13
  200.2 0.0 all-gather.14.cloned.1.call-update
  200.2 0.0 reduce-scatter.5.cloned.1.call-start
  200.2 11.7 %collective-permute-done.2 = bf16[192,2,384]{0,2,1:T(8,128)(2,1)S(1)} collective-permute-done((bf16[192,2,384]{0,2,1:T(8,128)(2,1)S(1)}, bf16[192,2,384]{0,2,1:T(8,128)(2,1)S(1)}, u32[]{:S(2)}, u32[]{:S(2)}) %collective-permute-start.2) | collective-permute-done | bytes 294944 | tf_op jit(solution)/shard_map/ppermute | solution.py:13
  211.9 15.5 %collective-permute-done.3 = bf16[192,2,384]{0,2,1:T(8,128)(2,1)S(1)} collective-permute-done((bf16[192,2,384]{0,2,1:T(8,128)(2,1)S(1)}, bf16[192,2,384]{0,2,1:T(8,128)(2,1)S(1)}, u32[]{:S(2)}, u32[]{:S(2)}) %collective-permute-start.3) | collective-permute-done | bytes 294944 | tf_op jit(solution)/shard_map/ppermute | solution.py:13
  227.5 0.7 convert_reduce_fusion.34
  228.2 20.3 %collective-permute-done.4 = bf16[192,2,384]{0,2,1:T(8,128)(2,1)S(1)} collective-permute-done((bf16[192,2,384]{0,2,1:T(8,128)(2,1)S(1)}, bf16[192,2,384]{0,2,1:T(8,128)(2,1)S(1)}, u32[]{:S(2)}, u32[]{:S(2)}) %collective-permute-start.4) | collective-permute-done | bytes 294944 | tf_op jit(solution)/shard_map/ppermute | solution.py:13
  248.5 0.1 convert_reduce_fusion.2
  248.6 0.7 slice_compare_fusion.29
  249.3 10.0 %collective-permute-done.5 = bf16[192,2,384]{0,2,1:T(8,128)(2,1)S(1)} collective-permute-done((bf16[192,2,384]{0,2,1:T(8,128)(2,1)S(1)}, bf16[192,2,384]{0,2,1:T(8,128)(2,1)S(1)}, u32[]{:S(2)}, u32[]{:S(2)}) %collective-permute-start.5) | collective-permute-done | bytes 294944 | tf_op jit(solution)/shard_map/ppermute | solution.py:13
  259.3 1.6 convert_reduce_fusion.33
  260.9 0.7 slice_compare_fusion.30
  261.6 8.1 %collective-permute-done.6 = bf16[192,2,384]{0,2,1:T(8,128)(2,1)S(1)} collective-permute-done((bf16[192,2,384]{0,2,1:T(8,128)(2,1)S(1)}, bf16[192,2,384]{0,2,1:T(8,128)(2,1)S(1)}, u32[]{:S(2)}, u32[]{:S(2)}) %collective-permute-start.6) | collective-permute-done | bytes 294944 | tf_op jit(solution)/shard_map/ppermute | solution.py:13
  269.7 8.1 %concatenate.6 = bf16[3072,2,384]{0,2,1:T(8,128)(2,1)} concatenate(bf16[192,2,384]{0,2,1:T(8,128)(2,1)S(1)} %collective-permute-done.6, bf16[192,2,384]{0,2,1:T(8,128)(2,1)S(1)} %collective-permute-done.5, bf16[192,2,384]{0,2,1:T(8,128)(2,1)S(1)} %collective-permute-done.4, bf16[192,2,384]{0,2,1:T(8,128)(2,1)S(1)} %collective-permute-done.3, ...), dimensions={0} | concatenate | bytes 9437184 | tf_op jit(solution)/shard_map/jit(_roll_dynamic)/concatenate | solution.py:16
  277.8 3.7 %fusion.2 = f32[512,2,384]{2,0,1:T(8,128)S(1)} fusion(bf16[3072,2,384]{0,2,1:T(8,128)(2,1)} %concatenate.6, s32[]{:T(128)S(6)} %select_n.114, bf16[512,1536]{1,0:T(8,128)(2,1)} %all-gather.12.cloned.1.call-done), kind=kOutput, calls=%fused_computation.8 | convolution fusion | flops 1207959552 | bytes 5505028 | tf_op jit(solution)/shard_map/dot_general | solution.py:114
  281.9 0.2 fusion.33
  282.1 0.0 all-gather.14.cloned.1.call-done
  282.2 0.0 copy-done.4
  282.2 0.0 copy-done.6
  282.2 0.0 copy-done.10
  282.3 0.0 copy-done.18
  282.3 0.0 copy-done.19
  282.4 0.0 copy-done.24
  282.4 0.0 copy-done.25
  282.4 0.0 copy-done.30
  282.5 0.0 copy-done.33
  282.5 0.0 copy-done.36
  282.5 0.0 copy-done.40
  282.6 10.5 %convolution_convert_fusion.1 = bf16[512,1536]{1,0:T(8,128)(2,1)} fusion(bf16[384,1536]{0,1:T(8,128)(2,1)} %all-gather.14.cloned.1.call-done, bf16[512,384]{1,0:T(8,128)(2,1)S(1)} %fusion.33, f32[384]{0:T(512)S(1)} %copy-done.30, f32[384]{0:T(512)S(1)} %copy-done.31, f32[384]{0:T(512)S(1)} %get-tuple-element.18, f32[384]{0:T(512)S(1)} %get-tuple-element.19, ...), kind=kOutput, calls=%fused_computation.6 | convolution fusion | flops 629932032 | bytes 3209216 | tf_op jit(solution)/shard_map/dot_general | solution.py:125
  293.1 0.0 reduce-scatter.5.cloned.1.call-update
  293.1 25.3 %reduce-scatter.5.cloned.1.call-done = bf16[128,1536]{1,0:T(8,128)(2,1)} async-done(((bf16[512,1536]{1,0:T(8,128)(2,1)}), bf16[128,1536]{1,0:T(8,128)(2,1)}) %reduce-scatter.5.cloned.1.call-update) | async-done | bytes 393232 | tf_op jit(solution)/shard_map/reduce_scatter | solution.py:124
  318.4 1.8 fusion.32
  (92 shorter events, 0.3 us)
Async XLA Ops:
  6.5 6.0 %copy-start.44 = (s32[1,4]{1,0:T(1,128)S(1)}, s32[1,4]{1,0:T(1,128)}, u32[]{:S(2)}) copy-start(s32[1,4]{1,0:T(1,128)} %param.10) | copy-start | bytes 52
  6.5 70.9 %all-gather.8.cloned.1.call-start = ((), (), s32[]{:S(2)}) async-start(), calls=%async_computation.3 | async-start | bytes 3981312 | tf_op jit(solution)/shard_map/all_gather | solution.py:81
  7.3 89.9 %all-gather.6.cloned.1.call-start = ((), (), s32[]{:S(2)}) async-start(), calls=%async_computation.2 | async-start | bytes 1966080 | tf_op jit(solution)/shard_map/all_gather | solution.py:93
  11.8 128.7 %all-gather.10.cloned.1.call-start = ((), (), s32[]{:S(2)}) async-start(), calls=%async_computation.4 | async-start | bytes 1327104 | tf_op jit(solution)/shard_map/all_gather | solution.py:82
  12.5 158.6 %reduce-scatter.3.cloned.1.call-start = ((), (), s32[]{:S(2)}) async-start(), calls=%async_computation.5 | async-start | bytes 1966080 | tf_op jit(solution)/shard_map/reduce_scatter | solution.py:102
  143.9 27.1 %copy-start = (bf16[1,128,1536]{2,1,0:T(8,128)(2,1)S(1)}, bf16[1,128,1536]{2,1,0:T(8,128)(2,1)}, u32[]{:S(2)}) copy-start(bf16[1,128,1536]{2,1,0:T(8,128)(2,1)} %param.9) | copy-start | bytes 1179652
  143.9 28.6 %copy-start.3 = (f32[1536]{0:T(1024)S(1)}, f32[1536]{0:T(1024)}, u32[]{:S(2)}) copy-start(f32[1536]{0:T(1024)} %param.12) | copy-start | bytes 18436
  144.0 29.7 %copy-start.1 = (bf16[192,2,384]{2,1,0:T(2,128)(2,1)S(1)}, bf16[192,2,384]{2,1,0:T(2,128)(2,1)}, u32[]{:S(2)}) copy-start(bf16[192,2,384]{2,1,0:T(2,128)(2,1)} %param.15) | copy-start | bytes 884740
  144.0 83.5 %copy-start.2 = (bf16[31,384]{1,0:T(8,128)(2,1)S(1)}, bf16[31,384]{1,0:T(8,128)(2,1)}, u32[]{:S(2)}) copy-start(bf16[31,384]{1,0:T(8,128)(2,1)} %param.16) | copy-start | bytes 71428
  144.0 133.8 %all-gather.12.cloned.1.call-start = ((), (), s32[]{:S(2)}) async-start(), calls=%async_computation.6 | async-start | bytes 1966080 | tf_op jit(solution)/shard_map/all_gather | solution.py:113
  173.6 108.5 %all-gather.14.cloned.1.call-start = ((), (), s32[]{:S(2)}) async-start(), calls=%async_computation.7 | async-start | bytes 1327104 | tf_op jit(solution)/shard_map/all_gather | solution.py:84
  173.9 13.6 %collective-permute-start = (bf16[192,2,384]{0,2,1:T(8,128)(2,1)S(1)}, bf16[192,2,384]{0,2,1:T(8,128)(2,1)S(1)}, u32[]{:S(2)}, u32[]{:S(2)}) collective-permute-start(bf16[192,2,384]{0,2,1:T(8,128)(2,1)S(1)} %copy.29), channel_id=1, source_target_pairs={{0,4},{4,8},{8,12},{12,16},{16,20},{20,24},{24,28},{28,0},{1,5},{5... | collective-permute-start | bytes 884744 | tf_op jit(solution)/shard_map/ppermute | solution.py:13
  187.5 12.7 %collective-permute-start.1 = (bf16[192,2,384]{0,2,1:T(8,128)(2,1)S(1)}, bf16[192,2,384]{0,2,1:T(8,128)(2,1)S(1)}, u32[]{:S(2)}, u32[]{:S(2)}) collective-permute-start(bf16[192,2,384]{0,2,1:T(8,128)(2,1)S(1)} %collective-permute-done), channel_id=1, source_target_pairs={{0,4},{4,8},{8,12},{12,16},{16,20},{20,24},{24,28},{28,0},{1,5},{5... | collective-permute-start | bytes 884744 | tf_op jit(solution)/shard_map/ppermute | solution.py:13
  200.2 11.8 %collective-permute-start.2 = (bf16[192,2,384]{0,2,1:T(8,128)(2,1)S(1)}, bf16[192,2,384]{0,2,1:T(8,128)(2,1)S(1)}, u32[]{:S(2)}, u32[]{:S(2)}) collective-permute-start(bf16[192,2,384]{0,2,1:T(8,128)(2,1)S(1)} %collective-permute-done.1), channel_id=1, source_target_pairs={{0,4},{4,8},{8,12},{12,16},{16,20},{20,24},{24,28},{28,0},{1,5},{5... | collective-permute-start | bytes 884744 | tf_op jit(solution)/shard_map/ppermute | solution.py:13
  200.2 118.2 %reduce-scatter.5.cloned.1.call-start = ((), (), s32[]{:S(2)}) async-start(), calls=%async_computation.8 | async-start | bytes 1966080 | tf_op jit(solution)/shard_map/reduce_scatter | solution.py:124
  211.9 15.5 %collective-permute-start.3 = (bf16[192,2,384]{0,2,1:T(8,128)(2,1)S(1)}, bf16[192,2,384]{0,2,1:T(8,128)(2,1)S(1)}, u32[]{:S(2)}, u32[]{:S(2)}) collective-permute-start(bf16[192,2,384]{0,2,1:T(8,128)(2,1)S(1)} %collective-permute-done.2), channel_id=1, source_target_pairs={{0,4},{4,8},{8,12},{12,16},{16,20},{20,24},{24,28},{28,0},{1,5},{5... | collective-permute-start | bytes 884744 | tf_op jit(solution)/shard_map/ppermute | solution.py:13
  227.5 21.0 %collective-permute-start.4 = (bf16[192,2,384]{0,2,1:T(8,128)(2,1)S(1)}, bf16[192,2,384]{0,2,1:T(8,128)(2,1)S(1)}, u32[]{:S(2)}, u32[]{:S(2)}) collective-permute-start(bf16[192,2,384]{0,2,1:T(8,128)(2,1)S(1)} %collective-permute-done.3), channel_id=1, source_target_pairs={{0,4},{4,8},{8,12},{12,16},{16,20},{20,24},{24,28},{28,0},{1,5},{5... | collective-permute-start | bytes 884744 | tf_op jit(solution)/shard_map/ppermute | solution.py:13
  248.5 10.8 %collective-permute-start.5 = (bf16[192,2,384]{0,2,1:T(8,128)(2,1)S(1)}, bf16[192,2,384]{0,2,1:T(8,128)(2,1)S(1)}, u32[]{:S(2)}, u32[]{:S(2)}) collective-permute-start(bf16[192,2,384]{0,2,1:T(8,128)(2,1)S(1)} %collective-permute-done.4), channel_id=1, source_target_pairs={{0,4},{4,8},{8,12},{12,16},{16,20},{20,24},{24,28},{28,0},{1,5},{5... | collective-permute-start | bytes 884744 | tf_op jit(solution)/shard_map/ppermute | solution.py:13
  259.3 10.5 %collective-permute-start.6 = (bf16[192,2,384]{0,2,1:T(8,128)(2,1)S(1)}, bf16[192,2,384]{0,2,1:T(8,128)(2,1)S(1)}, u32[]{:S(2)}, u32[]{:S(2)}) collective-permute-start(bf16[192,2,384]{0,2,1:T(8,128)(2,1)S(1)} %collective-permute-done.5), channel_id=1, source_target_pairs={{0,4},{4,8},{8,12},{12,16},{16,20},{20,24},{24,28},{28,0},{1,5},{5... | collective-permute-start | bytes 884744 | tf_op jit(solution)/shard_map/ppermute | solution.py:13
  281.5 0.7 copy-start.4
  281.5 0.7 copy-start.5
  281.5 0.7 copy-start.6
  281.5 0.7 copy-start.7
  281.5 0.7 copy-start.8
  281.6 0.7 copy-start.9
  281.6 0.7 copy-start.10
  281.6 0.7 copy-start.11
  281.6 0.7 copy-start.12
  281.6 0.7 copy-start.13
  281.6 0.7 copy-start.14
  281.6 0.7 copy-start.15
  281.6 0.7 copy-start.16
  281.6 0.7 copy-start.17
  281.6 0.7 copy-start.18
  281.7 0.7 copy-start.19
  281.7 0.7 copy-start.20
  281.7 0.7 copy-start.21
  281.7 0.7 copy-start.22
  281.7 0.7 copy-start.23
  281.7 0.7 copy-start.24
  281.7 0.7 copy-start.25
  281.7 0.7 copy-start.26
  281.7 0.7 copy-start.27
  281.7 0.7 copy-start.28
  281.8 0.7 copy-start.29
  281.8 0.7 copy-start.30
  281.8 0.7 copy-start.31
  281.8 0.7 copy-start.32
  281.8 0.7 copy-start.33
  281.8 0.7 copy-start.34
  281.8 0.7 copy-start.35
  281.8 0.7 copy-start.36
  281.8 0.7 copy-start.37
  281.8 0.7 copy-start.38
  281.9 0.7 copy-start.39
  281.9 0.7 copy-start.40
  281.9 0.7 copy-start.41
  281.9 0.7 copy-start.42
  281.9 0.7 copy-start.43
Sparse Core Ops, SparseCore 0:
  9.5 67.8 all-gather.7
  79.0 18.1 all-gather.5
  99.4 41.0 all-gather.9
  144.1 26.9 reduce-scatter.2
  173.7 19.6 all-gather.11
  200.3 47.9 all-gather.13
  293.2 25.1 reduce-scatter.4
